TPU v7x, 256 devices: a whole 4x4x8 slice. The times are simulated.
256 devices in a mesh: pix: 32 (over z, x), feat: 8 (over y, core).
Axes of the slice: x: 4, y: 4, z: 8, core: 2. Of those that a mesh axis runs over, the one named last changes fastest.
Arguments:
- mass_bin: int32 [262144, 256], P(('pix', 'feat')), may hold values from 0 to 255
- mobility_bin: int32 [262144, 256], P(('pix', 'feat')), may hold values from 0 to 15
- intensity: bfloat16 [262144, 256], P(('pix', 'feat')), may hold values from 10 to 4000, as said below
- basis_init: float32 [262144, 64], P(('pix', 'feat')), may hold values from 0.1 to 1
- profile_init: float32 [64, 4096], P(None, 'feat'), may hold values from 0.1 to 1
Outputs:
- basis: float32 [262144, 64], P(('pix', 'feat'))
- profiles: float32 [64, 4096], P(None, 'feat')
Inputs may be any that keep to these rules, and one draw needn't show every extreme that they name: `intensity`: positive peak intensities.
All inputs are finite; a program needn't handle non-finite values.
Results may differ from a plain program's by a relative error of at most 0.00045.
Values may be sent and summed in bfloat16 or wider, within the bound.
No kernel may reach another device: no remote copies, remote signals or barrier semaphores. Data moves between devices by JAX's collectives and lax.ppermute only.
A program may use at most 64 MiB of HBM per device.

v0:
```python
import math
import jax
import jax.numpy as jnp
from jax import lax
from jax.sharding import PartitionSpec as P

MZ = 256
MOB = 16
PEAKS = 256
ITERS = 2
EPS = 1e-06


def bin_block(args):
    mass, mobility, weight = args
    mass_hot = (mass[:, :, None] == jnp.arange(MZ, dtype=jnp.int32)[None, None, :]).astype(
        jnp.bfloat16
    ) * weight[:, :, None]
    mobility_hot = (mobility[:, :, None] == jnp.arange(MOB, dtype=jnp.int32)[None, None, :]).astype(
        jnp.bfloat16
    )
    dense = jnp.einsum("pkb,pkm->pbm", mobility_hot, mass_hot, preferred_element_type=jnp.float32)
    return dense.reshape(mass.shape[0], MZ * MOB).astype(jnp.bfloat16)


def local(mass_bin, mobility_bin, intensity, basis_init, profile_init):
    rows = mass_bin.shape[0]
    block = math.gcd(rows, 32)
    count = rows // block
    spectra = lax.map(
        bin_block,
        (
            mass_bin.reshape(count, block, PEAKS),
            mobility_bin.reshape(count, block, PEAKS),
            intensity.reshape(count, block, PEAKS),
        ),
    )
    spectra = spectra.reshape(rows, MZ * MOB)
    highest = lax.Precision.HIGHEST
    basis, profiles = (basis_init, profile_init)
    for step in range(ITERS):
        partial_h = lax.dot_general(
            basis.astype(jnp.bfloat16),
            spectra,
            (((0,), (0,)), ((), ())),
            preferred_element_type=jnp.float32,
        )
        partial_gram = lax.dot_general(
            basis,
            basis,
            (((0,), (0,)), ((), ())),
            precision=highest,
            preferred_element_type=jnp.float32,
        )
        shared = lax.psum_scatter(partial_h, "feat", scatter_dimension=1, tiled=True)
        numer_h = lax.psum(shared, "pix")
        gram_w = lax.psum(partial_gram, ("pix", "feat"))
        profiles = (
            profiles
            * numer_h
            / (
                jnp.dot(gram_w, profiles, precision=highest, preferred_element_type=jnp.float32)
                + EPS
            )
        )
        numer_w = lax.dot_general(
            spectra,
            lax.all_gather(profiles.astype(jnp.bfloat16), "feat", axis=1, tiled=True),
            (((1,), (1,)), ((), ())),
            preferred_element_type=jnp.float32,
        )
        local_gram = lax.dot_general(
            profiles,
            profiles,
            (((1,), (1,)), ((), ())),
            precision=highest,
            preferred_element_type=jnp.float32,
        )
        gram_h = lax.psum(local_gram, "feat")
        basis = (
            basis
            * numer_w
            / (jnp.dot(basis, gram_h, precision=highest, preferred_element_type=jnp.float32) + EPS)
        )
    return (basis, profiles)


def solution(mesh):
    return jax.shard_map(
        local,
        mesh=mesh,
        in_specs=(
            P(("pix", "feat"), None),
            P(("pix", "feat"), None),
            P(("pix", "feat"), None),
            P(("pix", "feat"), None),
            P(None, "feat"),
        ),
        out_specs=(P(("pix", "feat"), None), P(None, "feat")),
        check_vma=False,
    )
```

profile of v0, /device:TPU:2, one launch (start us, length us, event | category | flops | bytes accessed | tf_op | source)
XLA Modules:
  0.0 668.2 jit_solution(15157433333801755827)
XLA Ops:
  7.2 192.9 %while.10 = (s32[]{:T(128)}, bf16[32,32,4096]{2,1,0:T(8,128)(2,1)}, s32[32,32,256]{2,1,0:T(8,128)}, s32[32,32,256]{2,1,0:T(8,128)}, bf16[32,32,256]{2,1,0:T(8,128)(2,1)}, /*index=5*/s32[]{:T(128)}) while((s32[]{:T(128)}, bf16[32,32,4096]{2,1,0:T(8,128)(2,1)}, s32[32,32,256]{2,1,0:T(8,128)}, s32[32,32,256]{2,1,0:T(8,128)}, ...), condition=%wide.region_1.2_spmd, body=%wide.region_0.1_spmd.sunk | while | flops 71565312 | bytes 1557069 | solution.py:30
  8.8 3.7 fusion.50
  14.8 3.7 fusion.50
  20.8 3.7 fusion.50
  26.8 3.7 fusion.50
  32.9 3.7 fusion.50
  38.9 3.7 fusion.50
  44.9 3.7 fusion.50
  51.0 3.7 fusion.50
  57.0 3.7 fusion.50
  63.0 3.7 fusion.50
  69.0 3.7 fusion.50
  75.1 3.7 fusion.50
  81.1 3.7 fusion.50
  87.1 3.7 fusion.50
  93.2 3.7 fusion.50
  99.2 3.7 fusion.50
  105.2 3.7 fusion.50
  200.1 6.1 convolution_bitcast_fusion
  206.2 37.5 %reduce-scatter.3.cloned.1.call-done = f32[64,512]{1,0:T(8,128)} async-done(((f32[64,4096]{1,0:T(8,128)}), f32[64,512]{1,0:T(8,128)}) %reduce-scatter.3.cloned.1.call-update) | async-done | bytes 131088 | tf_op jit(solution)/shard_map/reduce_scatter | solution.py:55
  244.2 74.5 %psum.43 = f32[64,64]{1,0:T(8,128)S(1)} all-reduce(f32[64,64]{1,0:T(8,128)S(1)} %fusion.21), channel_id=1, replica_groups=mesh['pix'=32,'feat'=8] {'pix','feat'}, use_global_device_ids=true, to_apply=%region_4.5 | all-reduce | flops 4096 | bytes 32768 | tf_op jit(solution)/shard_map/psum | solution.py:57
  318.7 68.1 %all-reduce.3.cloned.1.call-done = f32[64,512]{1,0:T(8,128)} async-done(((f32[64,512]{1,0:T(8,128)}), f32[64,512]{1,0:T(8,128)}) %all-reduce.3.cloned.1.call-update) | async-done | bytes 131088 | tf_op jit(solution)/shard_map/psum | solution.py:56
  388.0 13.5 %all_gather.6 = bf16[64,4096]{1,0:T(8,128)(2,1)S(1)} all-gather(bf16[64,512]{1,0:T(8,128)(2,1)S(1)} %get-tuple-element.42), channel_id=1, replica_groups=mesh['pix'=32,'feat'=8] {'feat'}, dimensions={1}, use_global_device_ids=true | all-gather | bytes 589824 | tf_op jit(solution)/shard_map/all_gather | solution.py:68
  401.5 6.0 convolution_multiply_fusion.1
  407.8 25.8 %psum.44 = f32[64,64]{1,0:T(8,128)S(1)} all-reduce(f32[64,64]{1,0:T(8,128)S(1)} %fusion.22), channel_id=1, replica_groups=mesh['pix'=32,'feat'=8] {'feat'}, use_global_device_ids=true, to_apply=%region_5.6 | all-reduce | flops 4096 | bytes 32768 | tf_op jit(solution)/shard_map/psum | solution.py:79
  434.0 6.0 fusion.16
  440.1 30.4 %reduce-scatter.5.cloned.1.call-done = f32[64,512]{1,0:T(8,128)} async-done(((f32[64,4096]{1,0:T(8,128)}), f32[64,512]{1,0:T(8,128)}) %reduce-scatter.5.cloned.1.call-update) | async-done | bytes 131088 | tf_op jit(solution)/shard_map/reduce_scatter | solution.py:55
  470.8 74.4 %psum.46 = f32[64,64]{1,0:T(8,128)S(1)} all-reduce(f32[64,64]{1,0:T(8,128)S(1)} %fusion.23), channel_id=1, replica_groups=mesh['pix'=32,'feat'=8] {'pix','feat'}, use_global_device_ids=true, to_apply=%region_8.9 | all-reduce | flops 4096 | bytes 32768 | tf_op jit(solution)/shard_map/psum | solution.py:57
  545.2 68.6 %all-reduce.5.cloned.1.call-done = f32[64,512]{1,0:T(8,128)} async-done(((f32[64,512]{1,0:T(8,128)}), f32[64,512]{1,0:T(8,128)}) %all-reduce.5.cloned.1.call-update) | async-done | bytes 131088 | tf_op jit(solution)/shard_map/psum | solution.py:56
  615.0 13.4 %all_gather.7 = bf16[64,4096]{1,0:T(8,128)(2,1)S(1)} all-gather(bf16[64,512]{1,0:T(8,128)(2,1)S(1)} %get-tuple-element.44), channel_id=1, replica_groups=mesh['pix'=32,'feat'=8] {'feat'}, dimensions={1}, use_global_device_ids=true | all-gather | bytes 589824 | tf_op jit(solution)/shard_map/all_gather | solution.py:68
  628.5 6.0 convolution_multiply_fusion
  634.8 25.8 %psum.47 = f32[64,64]{1,0:T(8,128)S(1)} all-reduce(f32[64,64]{1,0:T(8,128)S(1)} %fusion.24), channel_id=1, replica_groups=mesh['pix'=32,'feat'=8] {'feat'}, use_global_device_ids=true, to_apply=%region_9.10 | all-reduce | flops 4096 | bytes 32768 | tf_op jit(solution)/shard_map/psum | solution.py:79
  (166 shorter events, 135.7 us)
Async XLA Ops:
  7.2 236.6 %reduce-scatter.3.cloned.1.call-start = ((), (), s32[]{:S(2)}) async-start(), calls=%async_computation.2 | async-start | bytes 1179648 | tf_op jit(solution)/shard_map/reduce_scatter | solution.py:55
  7.2 192.9 %copy-start = (f32[1024,64]{0,1:T(8,128)S(1)}, f32[1024,64]{0,1:T(8,128)}, u32[]{:S(2)}) copy-start(f32[1024,64]{0,1:T(8,128)} %param.10) | copy-start | bytes 786436
  200.1 186.7 %copy-start.2 = (f32[64,512]{1,0:T(8,128)S(1)}, f32[64,512]{1,0:T(8,128)}, u32[]{:S(2)}) copy-start(f32[64,512]{1,0:T(8,128)} %param.11) | copy-start | bytes 393220
  206.2 180.6 %all-reduce.3.cloned.1.call-start = ((), (), s32[]{:S(2)}) async-start(), calls=%async_computation.3 | async-start | bytes 262144 | tf_op jit(solution)/shard_map/psum | solution.py:56
  243.8 226.7 %reduce-scatter.5.cloned.1.call-start = ((), (), s32[]{:S(2)}) async-start(), calls=%async_computation.4 | async-start | bytes 1179648 | tf_op jit(solution)/shard_map/reduce_scatter | solution.py:55
  440.0 173.8 %all-reduce.5.cloned.1.call-start = ((), (), s32[]{:S(2)}) async-start(), calls=%async_computation.5 | async-start | bytes 262144 | tf_op jit(solution)/shard_map/psum | solution.py:56
  615.0 46.7 %copy-start.1 = (f32[64,512]{1,0:T(8,128)}, f32[64,512]{1,0:T(8,128)S(1)}, u32[]{:S(2)}) copy-start(f32[64,512]{1,0:T(8,128)S(1)} %get-tuple-element.45) | copy-start | bytes 393220
Sparse Core Ops, SparseCore 0:
  206.3 37.3 reduce-scatter.2
  247.2 139.5 all-reduce.2
  440.1 30.2 reduce-scatter.4
  474.1 139.6 all-reduce.4
where the time goes:
time: 673 us; the launch traced here: 668 us
  blocking collectives  227 us (34%)
  waiting for transfers between devices  205 us (30%)
  matrix products  146 us (22%)
  local copies, waits for them, and re-layouts  75.5 us (11%)
  between operations  13.8 us (2%)
    psum x2, blocking collectives, local(): gram_w = lax.psum(partial_gram, ('pix', 'feat'))  149 us
    psum x2, waiting for transfers between devices, local(): numer_h = lax.psum(shared, 'pix')  137 us
    dot_general x32, matrix products, bin_block(): jnp.einsum('pkb,pkm->pbm', mobility_hot, mass_hot, preferred_element_type...  117 us
    reduce_scatter x2, waiting for transfers between devices, local(): lax.psum_scatter(partial_h, 'feat', scatter_dimension=1, tiled=True)  67.8 us
    psum x2, blocking collectives, local(): gram_h = lax.psum(local_gram, 'feat')  51.6 us
    all_gather x2, blocking collectives, local(): lax.all_gather(profiles.astype(jnp.bfloat16), 'feat', axis=1, tiled=True)  26.9 us
    eq x32, local copies, waits for them, and re-layouts, bin_block(): mass[:, :, None] == jnp.arange(MZ, dtype=jnp.int32)[None, None, :]  25 us
    dynamic_update_slice x32, local copies, waits for them, and re-layouts, local(): lax.map(bin_block, (mass_bin.reshape(count, block, PEAKS), mobility_bin.r...  23.4 us
  transfers between devices with their start and end apart: 4, of which 4 were waited for; matrix products, arithmetic and copies ran while one was open for 0% of the time, Pallas kernels for 0%

commit v1 on v0

--- a/solution.py
+++ b/solution.py
@@ -53,7 +53,7 @@
             preferred_element_type=jnp.float32,
         )
         shared = lax.psum_scatter(partial_h, "feat", scatter_dimension=1, tiled=True)
-        numer_h = lax.psum(shared, "pix")
+        numer_h = jnp.sum(lax.all_gather(shared, "pix"), axis=0)
         gram_w = lax.psum(partial_gram, ("pix", "feat"))
         profiles = (
             profiles

time: 673 us -> 555 us (0.82)
  waiting for transfers between devices: 205 us -> 82 us
    psum x2 -> x0, waiting for transfers between devices: 137 us -> none  [local(): numer_h = lax.psum(shared, 'pix')]
    all_gather x0 -> x2, waiting for transfers between devices: none -> 13.9 us  [local(): numer_h = jnp.sum(lax.all_gather(shared, 'pix'), axis=0)]
where the time goes in v1:
time: 555 us; the launch traced here: 550 us
  blocking collectives  228 us (41%)
  matrix products  145 us (26%)
  waiting for transfers between devices  82 us (15%)
  local copies, waits for them, and re-layouts  75.5 us (14%)
  between operations  13.9 us (3%)
    psum x2, blocking collectives, local(): gram_w = lax.psum(partial_gram, ('pix', 'feat'))  149 us
    dot_general x32, matrix products, bin_block(): jnp.einsum('pkb,pkm->pbm', mobility_hot, mass_hot, preferred_element_type...  117 us
    reduce_scatter x2, waiting for transfers between devices, local(): lax.psum_scatter(partial_h, 'feat', scatter_dimension=1, tiled=True)  68.1 us
    psum x2, blocking collectives, local(): gram_h = lax.psum(local_gram, 'feat')  51.6 us
    all_gather x2, blocking collectives, local(): lax.all_gather(profiles.astype(jnp.bfloat16), 'feat', axis=1, tiled=True)  27.1 us
    eq x32, local copies, waits for them, and re-layouts, bin_block(): mass[:, :, None] == jnp.arange(MZ, dtype=jnp.int32)[None, None, :]  25 us
    dynamic_update_slice x32, local copies, waits for them, and re-layouts, local(): lax.map(bin_block, (mass_bin.reshape(count, block, PEAKS), mobility_bin.r...  23.4 us
    mul x32, local copies, waits for them, and re-layouts, bin_block(): (mass[:, :, None] == jnp.arange(MZ, dtype=jnp.int32)[None, None, :]).asty...  23 us
  transfers between devices with their start and end apart: 4, of which 4 were waited for; matrix products, arithmetic and copies ran while one was open for 0% of the time, Pallas kernels for 0%

profile of v1, /device:TPU:2, one launch (start us, length us, event | category | flops | bytes accessed | tf_op | source)
XLA Modules:
  0.0 549.5 jit_solution(4222541035810572901)
XLA Ops:
  7.2 192.9 %while.10 = (s32[]{:T(128)}, bf16[32,32,4096]{2,1,0:T(8,128)(2,1)}, s32[32,32,256]{2,1,0:T(8,128)}, s32[32,32,256]{2,1,0:T(8,128)}, bf16[32,32,256]{2,1,0:T(8,128)(2,1)}, /*index=5*/s32[]{:T(128)}) while((s32[]{:T(128)}, bf16[32,32,4096]{2,1,0:T(8,128)(2,1)}, s32[32,32,256]{2,1,0:T(8,128)}, s32[32,32,256]{2,1,0:T(8,128)}, ...), condition=%wide.region_1.2_spmd, body=%wide.region_0.1_spmd.sunk | while | flops 71565312 | bytes 1557069 | solution.py:30
  8.8 3.7 fusion.50
  14.8 3.7 fusion.50
  20.8 3.7 fusion.50
  26.8 3.7 fusion.50
  32.9 3.7 fusion.50
  38.9 3.7 fusion.50
  44.9 3.7 fusion.50
  51.0 3.7 fusion.50
  57.0 3.7 fusion.50
  63.0 3.7 fusion.50
  69.0 3.7 fusion.50
  75.1 3.7 fusion.50
  81.1 3.7 fusion.50
  87.1 3.7 fusion.50
  93.2 3.7 fusion.50
  99.2 3.7 fusion.50
  105.2 3.7 fusion.50
  200.1 6.1 %convolution_bitcast_fusion = f32[64,4096]{1,0:T(8,128)} fusion(bf16[1024,4096]{1,0:T(8,128)(2,1)} %bitcast.44, f32[1024,64]{0,1:T(8,128)S(1)} %copy-done), kind=kOutput, calls=%fused_computation.14 | convolution fusion | flops 536936448 | bytes 9699328 | tf_op jit(solution)/shard_map/dot_general | solution.py:42
  206.2 37.5 %reduce-scatter.3.cloned.1.call-done = f32[64,512]{1,0:T(8,128)} async-done(((f32[64,4096]{1,0:T(8,128)}), f32[64,512]{1,0:T(8,128)}) %reduce-scatter.3.cloned.1.call-update) | async-done | bytes 131088 | tf_op jit(solution)/shard_map/reduce_scatter | solution.py:55
  244.2 74.7 %psum.28 = f32[64,64]{1,0:T(8,128)S(1)} all-reduce(f32[64,64]{1,0:T(8,128)S(1)} %fusion.21), channel_id=1, replica_groups=mesh['pix'=32,'feat'=8] {'pix','feat'}, use_global_device_ids=true, to_apply=%region_4.5 | all-reduce | flops 4096 | bytes 32768 | tf_op jit(solution)/shard_map/psum | solution.py:57
  318.9 6.9 %all-gather.5.cloned.1.call-done = f32[2048,512]{1,0:T(8,128)} async-done(((f32[64,512]{1,0:T(8,128)}), f32[2048,512]{1,0:T(8,128)}) %all-gather.5.cloned.1.call-update) | async-done | bytes 4194320 | tf_op jit(solution)/shard_map/all_gather | solution.py:56
  328.6 13.5 %all_gather.20 = bf16[64,4096]{1,0:T(8,128)(2,1)S(1)} all-gather(bf16[64,512]{1,0:T(8,128)(2,1)S(1)} %get-tuple-element.42), channel_id=1, replica_groups=mesh['pix'=32,'feat'=8] {'feat'}, dimensions={1}, use_global_device_ids=true | all-gather | bytes 589824 | tf_op jit(solution)/shard_map/all_gather | solution.py:68
  342.1 6.0 %convolution_multiply_fusion.1 = f32[1024,64]{0,1:T(8,128)S(1)} fusion(f32[1024,64]{0,1:T(8,128)S(1)} %copy-done, bf16[1024,4096]{1,0:T(8,128)(2,1)} %bitcast.45, bf16[64,4096]{1,0:T(8,128)(2,1)S(1)} %all_gather.20), kind=kOutput, calls=%fused_computation.21 | convolution fusion | flops 536936448 | bytes 9437184 | tf_op jit(solution)/shard_map/dot_general | solution.py:66
  348.4 25.8 %psum.29 = f32[64,64]{1,0:T(8,128)S(1)} all-reduce(f32[64,64]{1,0:T(8,128)S(1)} %fusion.22), channel_id=1, replica_groups=mesh['pix'=32,'feat'=8] {'feat'}, use_global_device_ids=true, to_apply=%region_5.6 | all-reduce | flops 4096 | bytes 32768 | tf_op jit(solution)/shard_map/psum | solution.py:79
  374.6 6.0 %fusion.16 = f32[64,4096]{1,0:T(8,128)} fusion(bf16[1024,4096]{1,0:T(8,128)(2,1)} %bitcast.46, f32[1024,64]{0,1:T(8,128)S(1)} %fusion.13), kind=kOutput, calls=%fused_computation.26 | convolution fusion | flops 536936448 | bytes 9699328 | tf_op jit(solution)/shard_map/dot_general | solution.py:42
  380.7 30.6 %reduce-scatter.5.cloned.1.call-done = f32[64,512]{1,0:T(8,128)} async-done(((f32[64,4096]{1,0:T(8,128)}), f32[64,512]{1,0:T(8,128)}) %reduce-scatter.5.cloned.1.call-update) | async-done | bytes 131088 | tf_op jit(solution)/shard_map/reduce_scatter | solution.py:55
  411.7 74.6 %psum.30 = f32[64,64]{1,0:T(8,128)S(1)} all-reduce(f32[64,64]{1,0:T(8,128)S(1)} %fusion.23), channel_id=1, replica_groups=mesh['pix'=32,'feat'=8] {'pix','feat'}, use_global_device_ids=true, to_apply=%region_8.9 | all-reduce | flops 4096 | bytes 32768 | tf_op jit(solution)/shard_map/psum | solution.py:57
  486.3 6.9 %all-gather.7.cloned.1.call-done = f32[2048,512]{1,0:T(8,128)} async-done(((f32[64,512]{1,0:T(8,128)}), f32[2048,512]{1,0:T(8,128)}) %all-gather.7.cloned.1.call-update) | async-done | bytes 4194320 | tf_op jit(solution)/shard_map/all_gather | solution.py:56
  496.1 13.7 %all_gather.23 = bf16[64,4096]{1,0:T(8,128)(2,1)S(1)} all-gather(bf16[64,512]{1,0:T(8,128)(2,1)S(1)} %get-tuple-element.44), channel_id=1, replica_groups=mesh['pix'=32,'feat'=8] {'feat'}, dimensions={1}, use_global_device_ids=true | all-gather | bytes 589824 | tf_op jit(solution)/shard_map/all_gather | solution.py:68
  509.8 6.0 %convolution_multiply_fusion = f32[1024,64]{0,1:T(8,128)S(1)} fusion(f32[1024,64]{0,1:T(8,128)S(1)} %fusion.13, bf16[1024,4096]{1,0:T(8,128)(2,1)} %bitcast.47, bf16[64,4096]{1,0:T(8,128)(2,1)S(1)} %all_gather.23), kind=kOutput, calls=%fused_computation.20 | convolution fusion | flops 536936448 | bytes 9437184 | tf_op jit(solution)/shard_map/dot_general | solution.py:66
  516.1 25.8 %psum.31 = f32[64,64]{1,0:T(8,128)S(1)} all-reduce(f32[64,64]{1,0:T(8,128)S(1)} %fusion.24), channel_id=1, replica_groups=mesh['pix'=32,'feat'=8] {'feat'}, use_global_device_ids=true, to_apply=%region_9.10 | all-reduce | flops 4096 | bytes 32768 | tf_op jit(solution)/shard_map/psum | solution.py:79
  (168 shorter events, 139.0 us)
Async XLA Ops:
  7.2 236.6 %reduce-scatter.3.cloned.1.call-start = ((), (), s32[]{:S(2)}) async-start(), calls=%async_computation.2 | async-start | bytes 1179648 | tf_op jit(solution)/shard_map/reduce_scatter | solution.py:55
  7.2 192.9 %copy-start = (f32[1024,64]{0,1:T(8,128)S(1)}, f32[1024,64]{0,1:T(8,128)}, u32[]{:S(2)}) copy-start(f32[1024,64]{0,1:T(8,128)} %param.10) | copy-start | bytes 786436
  200.1 128.2 %copy-start.2 = (f32[64,512]{1,0:T(8,128)S(1)}, f32[64,512]{1,0:T(8,128)}, u32[]{:S(2)}) copy-start(f32[64,512]{1,0:T(8,128)} %param.11) | copy-start | bytes 393220
  206.2 119.6 %all-gather.5.cloned.1.call-start = ((), (), s32[]{:S(2)}) async-start(), calls=%async_computation.4 | async-start | bytes 4325376 | tf_op jit(solution)/shard_map/all_gather | solution.py:56
  243.8 167.6 %reduce-scatter.5.cloned.1.call-start = ((), (), s32[]{:S(2)}) async-start(), calls=%async_computation.3 | async-start | bytes 1179648 | tf_op jit(solution)/shard_map/reduce_scatter | solution.py:55
  380.6 112.6 %all-gather.7.cloned.1.call-start = ((), (), s32[]{:S(2)}) async-start(), calls=%async_computation.5 | async-start | bytes 4325376 | tf_op jit(solution)/shard_map/all_gather | solution.py:56
  496.1 46.9 %copy-start.1 = (f32[64,512]{1,0:T(8,128)}, f32[64,512]{1,0:T(8,128)S(1)}, u32[]{:S(2)}) copy-start(f32[64,512]{1,0:T(8,128)S(1)} %get-tuple-element.45) | copy-start | bytes 393220
Sparse Core Ops, SparseCore 0:
  206.3 37.3 reduce-scatter.2
  246.3 79.4 all-gather.4
  380.8 30.5 reduce-scatter.4
  413.8 79.4 all-gather.6
